TPU v7x, 256 devices: a whole 4x4x8 slice. The times are simulated.
256 devices in a mesh: row: 16 (over z, y_hi), col: 16 (over x, y_lo, core).
Axes of the slice: x: 4, y: 4 (y_hi: 2, y_lo: 2; y = y_hi * 2 + y_lo), z: 8, core: 2. Of those that a mesh axis runs over, the one named last changes fastest.
Arguments:
- queries: bfloat16 [32, 2048, 128], P('row', 'col'), may hold values from -6.5 to 6.5
- keys: bfloat16 [32, 2048, 128], P('row', 'col'), may hold values from -6.5 to 6.5
- values: bfloat16 [32, 2048, 128], P('row', 'col'), may hold values from -6 to 6
- gate: bfloat16 [32, 2048, 128], P('row', 'col'), may hold values from -6 to 6
- bias: bfloat16 [4, 2048, 2048], P(None, 'col'), may hold values from -7.5 to 7.5
- grad_out: bfloat16 [32, 2048, 128], P('row', 'col'), may hold values from -6 to 6
- block_mask: int32 [16, 16], replicated, may hold values from 0 to 1, as said below
Outputs:
- query_grad: bfloat16 [32, 2048, 128], P('row', 'col')
- key_grad: bfloat16 [32, 2048, 128], P('row', 'col')
- value_grad: bfloat16 [32, 2048, 128], P('row', 'col')
- gate_grad: bfloat16 [32, 2048, 128], P('row', 'col')
- bias_grad: float32 [4, 2048, 2048], P(None, 'col', 'row')
Inputs may be any that keep to these rules, and one draw needn't show every extreme that they name: `block_mask`: every diagonal block is 1.
All inputs are finite; a program needn't handle non-finite values.
Results may differ from a plain program's by a relative error of at most 0.02.
Values may be sent and summed in bfloat16 or wider, within the bound.
No kernel may reach another device: no remote copies, remote signals or barrier semaphores. Data moves between devices by JAX's collectives and lax.ppermute only.
A program may use at most 64 MiB of HBM per device.

v0:
```python
import math
import jax
import jax.numpy as jnp
from jax import lax
from jax.sharding import PartitionSpec as P

H = 4
DH = 32
BLK = 128
NEGATIVE = -1000000000.0


def block_flags(block_mask, first_row, row_count, key_block):
    block_ids = (first_row + jnp.arange(row_count, dtype=jnp.int32)) // BLK
    column = lax.dynamic_index_in_dim(block_mask, key_block, axis=1, keepdims=False)
    matching = block_ids[:, None] == jnp.arange(block_mask.shape[0], dtype=jnp.int32)[None, :]
    return jnp.sum(jnp.where(matching, column[None, :], 0), axis=1) > 0


def tile_scores(query_tile, key_tile, bias_tile, allowed, score_scale):
    products = jnp.einsum(
        "rjhd,rkhd->rhjk", query_tile, key_tile, preferred_element_type=jnp.float32
    )
    scores = products * score_scale + bias_tile.astype(jnp.float32)[None]
    return jnp.where(allowed[None, None, :, None], scores, NEGATIVE)


def tile_grads(
    query_tile, key_tile, value_tile, bias_tile, allowed, log_total, grad_dot, out_grad, score_scale
):
    scores = tile_scores(query_tile, key_tile, bias_tile, allowed, score_scale)
    weights = jnp.exp(scores - log_total[..., None])
    prob_grad = jnp.einsum(
        "rjhd,rkhd->rhjk", out_grad, value_tile, preferred_element_type=jnp.float32
    )
    return (weights, weights * (prob_grad - grad_dot[..., None]))


def local(queries, keys, values, gate, bias, grad_out, block_mask):
    slab_rows, local_cols, channels = queries.shape
    head_count = H
    head_size = DH
    score_scale = 1.0 / math.sqrt(head_size)
    col_start = lax.axis_index("col") * local_cols
    key_all, value_all = (
        lax.all_gather(keys, "col", axis=1, tiled=True),
        lax.all_gather(values, "col", axis=1, tiled=True),
    )
    all_cols = key_all.shape[1]
    blocks = all_cols // BLK
    query_heads = queries.reshape(slab_rows, local_cols, head_count, head_size)
    key_heads_all = key_all.reshape(slab_rows, all_cols, head_count, head_size)
    value_heads_all = value_all.reshape(slab_rows, all_cols, head_count, head_size)

    def key_slices(key_block):
        offset = key_block * BLK
        return (
            lax.dynamic_slice_in_dim(key_heads_all, offset, BLK, 1),
            lax.dynamic_slice_in_dim(value_heads_all, offset, BLK, 1),
            lax.dynamic_slice_in_dim(bias, offset, BLK, 2),
            block_flags(block_mask, col_start, local_cols, key_block),
        )

    def stats_step(key_block, carried):
        key_tile, value_tile, bias_tile, allowed = key_slices(key_block)

        def stats_update(state_in):
            row_top, row_mass = state_in
            scores = tile_scores(query_heads, key_tile, bias_tile, allowed, score_scale)
            new_top = jnp.maximum(row_top, jnp.max(scores, axis=3))
            row_mass = row_mass * jnp.exp(row_top - new_top) + jnp.sum(
                jnp.exp(scores - new_top[..., None]), axis=3
            )
            return (new_top, row_mass)

        return lax.cond(jnp.any(allowed), stats_update, lambda kept: kept, carried)

    stat_shape = (slab_rows, head_count, local_cols)
    row_top, row_mass = lax.fori_loop(
        0,
        blocks,
        stats_step,
        (jnp.full(stat_shape, -1e30, jnp.float32), jnp.zeros(stat_shape, jnp.float32)),
    )
    log_total = row_top + jnp.log(row_mass)

    def attend_step(key_block, carried):
        key_tile, value_tile, bias_tile, allowed = key_slices(key_block)

        def attend_update(running):
            scores = tile_scores(query_heads, key_tile, bias_tile, allowed, score_scale)
            probs = jnp.exp(scores - log_total[..., None]).astype(jnp.bfloat16)
            return running + jnp.einsum(
                "rhjk,rkhd->rjhd", probs, value_tile, preferred_element_type=jnp.float32
            )

        return lax.cond(jnp.any(allowed), attend_update, lambda kept: kept, carried)

    attended = lax.fori_loop(
        0,
        blocks,
        attend_step,
        jnp.zeros((slab_rows, local_cols, head_count, head_size), jnp.float32),
    )
    gate_sig = jax.nn.sigmoid(gate.astype(jnp.float32)).reshape(
        slab_rows, local_cols, head_count, head_size
    )
    cotangent = grad_out.astype(jnp.float32).reshape(slab_rows, local_cols, head_count, head_size)
    gate_grad = (
        (cotangent * attended * gate_sig * (1.0 - gate_sig))
        .astype(jnp.bfloat16)
        .reshape(slab_rows, local_cols, channels)
    )
    out_grad = (cotangent * gate_sig).astype(jnp.bfloat16)
    grad_dot = jnp.transpose(jnp.sum(out_grad.astype(jnp.float32) * attended, axis=3), (0, 2, 1))

    def grad_step(key_block, carried):
        key_tile, value_tile, bias_tile, allowed = key_slices(key_block)

        def grad_update(state_in):
            query_acc, bias_part, key_part, value_part = state_in
            weights, score_grad = tile_grads(
                query_heads,
                key_tile,
                value_tile,
                bias_tile,
                allowed,
                log_total,
                grad_dot,
                out_grad,
                score_scale,
            )
            score_grad_b = score_grad.astype(jnp.bfloat16)
            query_acc = query_acc + jnp.einsum(
                "rhjk,rkhd->rjhd", score_grad_b, key_tile, preferred_element_type=jnp.float32
            )
            offset = key_block * BLK
            bias_part = lax.dynamic_update_slice_in_dim(
                bias_part, jnp.sum(score_grad, axis=0), offset, 2
            )
            key_piece = jnp.einsum(
                "rhjk,rjhd->rkhd", score_grad_b, query_heads, preferred_element_type=jnp.float32
            )
            value_piece = jnp.einsum(
                "rhjk,rjhd->rkhd",
                weights.astype(jnp.bfloat16),
                out_grad,
                preferred_element_type=jnp.float32,
            )
            key_part = lax.dynamic_update_slice_in_dim(
                key_part, key_piece.reshape(slab_rows, BLK, channels), offset, 1
            )
            value_part = lax.dynamic_update_slice_in_dim(
                value_part, value_piece.reshape(slab_rows, BLK, channels), offset, 1
            )
            return (query_acc, bias_part, key_part, value_part)

        return lax.cond(jnp.any(allowed), grad_update, lambda kept: kept, carried)

    part_shape = (slab_rows, all_cols, channels)
    initial = (
        jnp.zeros((slab_rows, local_cols, head_count, head_size), jnp.float32),
        jnp.zeros((head_count, local_cols, all_cols), jnp.float32),
        jnp.zeros(part_shape, jnp.float32),
        jnp.zeros(part_shape, jnp.float32),
    )
    query_acc, bias_part, key_part, value_part = lax.fori_loop(0, blocks, grad_step, initial)
    key_sum, value_sum = (
        lax.psum_scatter(key_part, "col", scatter_dimension=1, tiled=True),
        lax.psum_scatter(value_part, "col", scatter_dimension=1, tiled=True),
    )
    key_grad = (key_sum * score_scale).astype(jnp.bfloat16)
    value_grad = value_sum.astype(jnp.bfloat16)
    bias_grad = lax.psum_scatter(bias_part, "row", scatter_dimension=2, tiled=True)
    query_grad = (
        (query_acc * score_scale).astype(jnp.bfloat16).reshape(slab_rows, local_cols, channels)
    )
    return (query_grad, key_grad, value_grad, gate_grad, bias_grad)


def solution(mesh):
    return jax.shard_map(
        local,
        mesh=mesh,
        in_specs=(
            P("row", "col", None),
            P("row", "col", None),
            P("row", "col", None),
            P("row", "col", None),
            P(None, "col", None),
            P("row", "col", None),
            P(),
        ),
        out_specs=(
            P("row", "col", None),
            P("row", "col", None),
            P("row", "col", None),
            P("row", "col", None),
            P(None, "col", "row"),
        ),
        check_vma=False,
    )
```

profile of v0, /device:TPU:4, one launch (start us, length us, event | category | flops | bytes accessed | tf_op | source)
XLA Modules:
  0.0 607.0 jit_solution(3435595489802957417)
XLA Ops:
  8.7 3.1 copy.84
  13.6 32.8 %all-gather.3.cloned.1.call-done = bf16[2,2048,128]{2,1,0:T(8,128)(2,1)} async-done(((bf16[2,128,128]{2,1,0:T(8,128)(2,1)}), bf16[2,2048,128]{2,1,0:T(8,128)(2,1)}) %all-gather.3.cloned.1.call-update) | async-done | bytes 1048592 | tf_op jit(solution)/shard_map/all_gather | solution.py:46
  48.0 26.1 %while.56 = (s32[]{:T(128)}, f32[2,4,128]{2,1,0:T(4,128)S(1)}, f32[2,4,128]{2,1,0:T(4,128)S(1)}, s32[]{:T(128)}, s32[16,16]{0,1:T(8,128)S(1)}, /*index=5*/bf16[2...) while((s32[]{:T(128)}, f32[2,4,128]{2,1,0:T(4,128)S(1)}, ...), condition=%wide.region_7.8_spmd, body=%wide.region_0.7_spmd.sunk | while | flops 9250950 | bytes 1891393 | solution.py:79
  74.1 9.0 %all-gather.5.cloned.1.call-done = bf16[2,2048,128]{2,1,0:T(8,128)(2,1)} async-done(((bf16[2,128,128]{2,1,0:T(8,128)(2,1)}), bf16[2,2048,128]{2,1,0:T(8,128)(2,1)}) %all-gather.5.cloned.1.call-update) | async-done | bytes 1048592 | tf_op jit(solution)/shard_map/all_gather | solution.py:47
  83.1 2.3 copy.78
  86.1 35.5 %while.57 = (s32[]{:T(128)}, f32[2,128,4,32]{1,3,2,0:T(8,128)}, s32[]{:T(128)}, s32[16,16]{0,1:T(8,128)S(1)}, bf16[2,2048,4,32]{1,3,2,0:T(8,128)(2,1)S(1)}, /*in...) while((s32[]{:T(128)}, f32[2,128,4,32]{1,3,2,0:T(8,128)}, ...), condition=%wide.region_13.14_spmd, body=%wide.region_8.13_spmd.sunk | while | flops 17539204 | bytes 1122349 | solution.py:99
  87.5 2.1 conditional.7
  87.5 2.1 fusion.14
  91.0 2.1 conditional.7
  91.0 2.1 fusion.14
  97.4 2.1 conditional.7
  97.4 2.1 fusion.14
  105.2 2.1 conditional.7
  105.3 2.1 fusion.14
  108.7 2.1 conditional.7
  108.8 2.1 fusion.14
  113.7 2.1 conditional.7
  113.7 2.1 fusion.14
  123.1 2.2 broadcast_in_dim.201
  127.1 50.5 %while.58 = (s32[]{:T(128)}, f32[2,128,4,32]{1,3,2,0:T(8,128)S(1)}, f32[4,128,2048]{1,2,0:T(8,128)}, f32[2,2048,128]{1,2,0:T(8,128)S(1)}, f32[2,2048,128]{1,2,0:...) while((s32[]{:T(128)}, f32[2,128,4,32]{1,3,2,0:T(8,128)S(1)}, ...), condition=%wide.region_21.22_spmd, body=%wide.region_15.21_spmd.sunk | while | flops 43163780 | bytes 5319889 | solution.py:167
  128.6 4.6 conditional.8
  134.6 4.6 conditional.8
  143.5 4.6 conditional.8
  153.9 4.6 conditional.8
  159.9 4.6 conditional.8
  167.3 4.6 conditional.8
  177.7 3.0 copy.86
  180.7 1.8 copy.85
  182.6 5.4 copy.87
  189.5 114.2 %reduce-scatter.6.cloned.1.call-done = f32[2,128,128]{2,1,0:T(8,128)} async-done(((f32[2,2048,128]{2,1,0:T(8,128)}), f32[2,128,128]{2,1,0:T(8,128)}) %reduce-scatter.6.cloned.1.call-update) | async-done | bytes 131088 | tf_op jit(solution)/shard_map/reduce_scatter | solution.py:170
  305.3 66.8 %reduce-scatter.4.cloned.1.call-done = f32[2,128,128]{2,1,0:T(8,128)} async-done(((f32[2,2048,128]{2,1,0:T(8,128)}), f32[2,128,128]{2,1,0:T(8,128)}) %reduce-scatter.4.cloned.1.call-update) | async-done | bytes 131088 | tf_op jit(solution)/shard_map/reduce_scatter | solution.py:169
  373.7 226.8 %reduce-scatter.8.cloned.1.call-done = f32[4,128,128]{2,1,0:T(8,128)} async-done(((f32[4,128,2048]{2,1,0:T(8,128)}), f32[4,128,128]{2,1,0:T(8,128)}) %reduce-scatter.8.cloned.1.call-update) | async-done | bytes 262160 | tf_op jit(solution)/shard_map/reduce_scatter | solution.py:174
  (357 shorter events, 82.6 us)
Async XLA Ops:
  7.2 39.3 %all-gather.3.cloned.1.call-start = ((), (), s32[]{:S(2)}) async-start(), calls=%async_computation.3 | async-start | bytes 1114112 | tf_op jit(solution)/shard_map/all_gather | solution.py:46
  7.9 75.2 %all-gather.5.cloned.1.call-start = ((), (), s32[]{:S(2)}) async-start(), calls=%async_computation.4 | async-start | bytes 1114112 | tf_op jit(solution)/shard_map/all_gather | solution.py:47
  8.7 295.1 %reduce-scatter.6.cloned.1.call-start = ((), (), s32[]{:S(2)}) async-start(), calls=%async_computation.6 | async-start | bytes 2228224 | tf_op jit(solution)/shard_map/reduce_scatter | solution.py:170
  8.7 3.1 copy-start.3
  8.7 3.3 copy-start.4
  8.7 3.3 copy-start.1
  8.7 4.1 copy-start.2
  121.6 1.6 copy-start
  180.7 191.4 %reduce-scatter.4.cloned.1.call-start = ((), (), s32[]{:S(2)}) async-start(), calls=%async_computation.5 | async-start | bytes 2228224 | tf_op jit(solution)/shard_map/reduce_scatter | solution.py:169
  182.6 417.9 %reduce-scatter.8.cloned.1.call-start = ((), (), s32[]{:S(2)}) async-start(), calls=%async_computation.7 | async-start | bytes 4456448 | tf_op jit(solution)/shard_map/reduce_scatter | solution.py:174
Sparse Core Ops, SparseCore 0:
  9.8 36.6 all-gather.2
  48.3 34.7 all-gather.4
  180.8 122.9 reduce-scatter.5
  306.2 65.8 reduce-scatter.3
  376.5 223.8 reduce-scatter.7
where the time goes:
time: 609 us; the launch traced here: 607 us
  waiting for transfers between devices  451 us (74%)
  other arithmetic  46.5 us (8%)
  local copies, waits for them, and re-layouts  34 us (6%)
  loops' own time  34 us (6%)
  matrix products  27.2 us (4%)
  between operations  13.9 us (2%)
    reduce_scatter x1, waiting for transfers between devices, local(): lax.psum_scatter(bias_part, 'row', scatter_dimension=2, tiled=True)  227 us
    reduce_scatter x1, waiting for transfers between devices, local(): lax.psum_scatter(value_part, 'col', scatter_dimension=1, tiled=True)  114 us
    reduce_scatter x1, waiting for transfers between devices, local(): lax.psum_scatter(key_part, 'col', scatter_dimension=1, tiled=True)  66.8 us
    all_gather x1, waiting for transfers between devices, local(): lax.all_gather(keys, 'col', axis=1, tiled=True)  32.8 us
    gt x48, other arithmetic, block_flags(): return jnp.sum(jnp.where(matching, column[None, :], 0), axis=1) > 0  30.5 us
    while x5, local copies, waits for them, and re-layouts, local(): lax.fori_loop(0, blocks, grad_step, initial)  13.3 us
    dot_general x6, matrix products, attend_update(): jnp.einsum('rhjk,rkhd->rjhd', probs, value_tile, preferred_element_type=j...  12.3 us
  transfers between devices with their start and end apart: 5, of which 5 were waited for; matrix products, arithmetic and copies ran while one was open for 5% of the time, Pallas kernels for 0%

commit v1 on v0

--- a/solution.py
+++ b/solution.py
@@ -43,7 +43,9 @@
     score_scale = 1.0 / math.sqrt(head_size)
     col_start = lax.axis_index("col") * local_cols
     key_all, value_all = (
-        lax.all_gather(keys, "col", axis=1, tiled=True),
+        jnp.concatenate(
+            lax.all_to_all(jnp.stack([keys] * lax.axis_size("col")), "col", 0, 0), axis=1
+        ),
         lax.all_gather(values, "col", axis=1, tiled=True),
     )
     all_cols = key_all.shape[1]

time: 609 us -> 590 us (0.969)
  waiting for transfers between devices: 451 us -> 422 us
    all_gather x1 -> x0, waiting for transfers between devices: 32.8 us -> none  [local(): lax.all_gather(keys, 'col', axis=1, tiled=True)]
    all_gather x1, waiting for transfers between devices: 9.01 us -> 0.02 us  [local(): lax.all_gather(values, 'col', axis=1, tiled=True)]
    all_to_all x0 -> x1, waiting for transfers between devices: none -> 8.46 us  [local(): lax.all_to_all(jnp.stack([keys] * lax.axis_size('col')), 'col', 0, 0)]
  transfers between devices with their start and end apart: 5 -> 5, of which waited for: 5 -> 4; matrix products, arithmetic and copies ran while one was open for 5% -> 6% of each run, Pallas kernels for 0% -> 0%
where the time goes in v1:
time: 590 us; the launch traced here: 588 us
  waiting for transfers between devices  422 us (72%)
  other arithmetic  46.5 us (8%)
  local copies, waits for them, and re-layouts  38 us (6%)
  loops' own time  34 us (6%)
  matrix products  27.2 us (5%)
  between operations  13.9 us (2%)
  starting transfers between devices  5.99 us (1%)
    reduce_scatter x1, waiting for transfers between devices, local(): lax.psum_scatter(bias_part, 'row', scatter_dimension=2, tiled=True)  227 us
    reduce_scatter x1, waiting for transfers between devices, local(): lax.psum_scatter(value_part, 'col', scatter_dimension=1, tiled=True)  120 us
    reduce_scatter x1, waiting for transfers between devices, local(): lax.psum_scatter(key_part, 'col', scatter_dimension=1, tiled=True)  66.5 us
    gt x48, other arithmetic, block_flags(): return jnp.sum(jnp.where(matching, column[None, :], 0), axis=1) > 0  30.5 us
    while x5, local copies, waits for them, and re-layouts, local(): lax.fori_loop(0, blocks, grad_step, initial)  13.3 us
    dot_general x6, matrix products, attend_update(): jnp.einsum('rhjk,rkhd->rjhd', probs, value_tile, preferred_element_type=j...  12.3 us
  transfers between devices with their start and end apart: 5, of which 4 were waited for; matrix products, arithmetic and copies ran while one was open for 6% of the time, Pallas kernels for 0%

profile of v1, /device:TPU:4, one launch (start us, length us, event | category | flops | bytes accessed | tf_op | source)
XLA Modules:
  0.0 587.9 jit_solution(86136132312958457)
XLA Ops:
  9.4 5.8 all-to-all-start
  16.1 3.1 copy.106
  20.9 8.5 %all-to-all-done = bf16[16,2,128,128]{2,3,1,0:T(8,128)(2,1)S(1)} async-done(((bf16[16,2,128,128]{2,3,1,0:T(8,128)(2,1)}), bf16[16,2,128,128]{2,3,1,0:T(8,128)(2,1)S(1)}, u32[]{:S(2)}, u32[]{:S(2)}) %all-to-all-start) | async-done | bytes 1048608 | tf_op jit(solution)/shard_map/all_to_all | solution.py:47
  32.7 26.1 %while.56 = (s32[]{:T(128)}, f32[2,4,128]{2,1,0:T(4,128)S(1)}, f32[2,4,128]{2,1,0:T(4,128)S(1)}, s32[]{:T(128)}, s32[16,16]{0,1:T(8,128)S(1)}, /*index=5*/bf16[2...) while((s32[]{:T(128)}, f32[2,4,128]{2,1,0:T(4,128)S(1)}, ...), condition=%wide.region_7.8_spmd, body=%wide.region_0.7_spmd.sunk | while | flops 9250950 | bytes 1891393 | solution.py:81
  58.8 2.3 copy.100
  61.8 35.5 %while.57 = (s32[]{:T(128)}, f32[2,128,4,32]{1,3,2,0:T(8,128)}, s32[]{:T(128)}, s32[16,16]{0,1:T(8,128)S(1)}, bf16[2,2048,4,32]{1,3,2,0:T(8,128)(2,1)S(1)}, /*in...) while((s32[]{:T(128)}, f32[2,128,4,32]{1,3,2,0:T(8,128)}, ...), condition=%wide.region_13.14_spmd, body=%wide.region_8.13_spmd.sunk | while | flops 17539204 | bytes 1122349 | solution.py:101
  63.2 2.1 conditional.7
  63.2 2.1 fusion.14
  66.7 2.1 conditional.7
  66.8 2.1 fusion.14
  73.1 2.1 conditional.7
  73.1 2.1 fusion.14
  80.9 2.1 conditional.7
  81.0 2.1 fusion.14
  84.4 2.1 conditional.7
  84.5 2.1 fusion.14
  89.4 2.1 conditional.7
  89.5 2.1 fusion.14
  98.8 2.2 broadcast_in_dim.201
  102.9 50.5 %while.58 = (s32[]{:T(128)}, f32[2,128,4,32]{1,3,2,0:T(8,128)S(1)}, f32[4,128,2048]{1,2,0:T(8,128)}, f32[2,2048,128]{1,2,0:T(8,128)S(1)}, f32[2,2048,128]{1,2,0:...) while((s32[]{:T(128)}, f32[2,128,4,32]{1,3,2,0:T(8,128)S(1)}, ...), condition=%wide.region_21.22_spmd, body=%wide.region_15.21_spmd.sunk | while | flops 43163780 | bytes 5319889 | solution.py:169
  104.3 4.6 conditional.8
  110.3 4.6 conditional.8
  119.2 4.6 conditional.8
  129.6 4.6 conditional.8
  135.6 4.6 conditional.8
  143.0 4.6 conditional.8
  153.4 3.0 copy.108
  156.5 1.8 copy.107
  158.3 5.4 copy.109
  165.3 120.0 %reduce-scatter.6.cloned.1.call-done = f32[2,128,128]{2,1,0:T(8,128)} async-done(((f32[2,2048,128]{2,1,0:T(8,128)}), f32[2,128,128]{2,1,0:T(8,128)}) %reduce-scatter.6.cloned.1.call-update) | async-done | bytes 131088 | tf_op jit(solution)/shard_map/reduce_scatter | solution.py:172
  286.8 66.5 %reduce-scatter.4.cloned.1.call-done = f32[2,128,128]{2,1,0:T(8,128)} async-done(((f32[2,2048,128]{2,1,0:T(8,128)}), f32[2,128,128]{2,1,0:T(8,128)}) %reduce-scatter.4.cloned.1.call-update) | async-done | bytes 131088 | tf_op jit(solution)/shard_map/reduce_scatter | solution.py:171
  354.8 226.5 %reduce-scatter.8.cloned.1.call-done = f32[4,128,128]{2,1,0:T(8,128)} async-done(((f32[4,128,2048]{2,1,0:T(8,128)}), f32[4,128,128]{2,1,0:T(8,128)}) %reduce-scatter.8.cloned.1.call-update) | async-done | bytes 262160 | tf_op jit(solution)/shard_map/reduce_scatter | solution.py:176
  (359 shorter events, 85.9 us)
Async XLA Ops:
  9.4 20.0 %all-to-all-start = ((bf16[16,2,128,128]{2,3,1,0:T(8,128)(2,1)}), bf16[16,2,128,128]{2,3,1,0:T(8,128)(2,1)S(1)}, u32[]{:S(2)}, u32[]{:S(2)}) async-start(bf16[16,2,128,128]{2,3,1,0:T(8,128)(2,1)} %stack.2), calls=%async_computation | async-start | bytes 2097152 | tf_op jit(solution)/shard_map/all_to_all | solution.py:47
  15.2 43.5 %all-gather.2.cloned.1.call-start = ((), (), s32[]{:S(2)}) async-start(), calls=%async_computation.4 | async-start | bytes 1114112 | tf_op jit(solution)/shard_map/all_gather | solution.py:49
  16.0 269.3 %reduce-scatter.6.cloned.1.call-start = ((), (), s32[]{:S(2)}) async-start(), calls=%async_computation.6 | async-start | bytes 2228224 | tf_op jit(solution)/shard_map/reduce_scatter | solution.py:172
  16.0 3.1 copy-start.3
  16.0 3.3 copy-start.4
  16.0 3.3 copy-start.1
  16.1 4.1 copy-start.2
  97.3 1.6 copy-start
  156.4 196.9 %reduce-scatter.4.cloned.1.call-start = ((), (), s32[]{:S(2)}) async-start(), calls=%async_computation.5 | async-start | bytes 2228224 | tf_op jit(solution)/shard_map/reduce_scatter | solution.py:171
  158.3 423.1 %reduce-scatter.8.cloned.1.call-start = ((), (), s32[]{:S(2)}) async-start(), calls=%async_computation.7 | async-start | bytes 4456448 | tf_op jit(solution)/shard_map/reduce_scatter | solution.py:176
Sparse Core Ops, SparseCore 0:
  17.8 36.4 all-gather.1
  156.5 128.6 reduce-scatter.5
  287.8 65.4 reduce-scatter.3
  357.7 223.5 reduce-scatter.7
